TPU v7x, 32 devices: a whole 2x2x4 slice. The times are simulated.
32 devices in a mesh: px: 4 (over y, x), py: 8 (over z, core).
Axes of the slice: x: 2, y: 2, z: 4, core: 2. Of those that a mesh axis runs over, the one named last changes fastest.
Arguments:
- residual: float32 [10, 2048, 2048], P(None, 'py', 'px'), may hold values from -6 to 6
- lambda_x: float32 [2048], P('px'), may hold values from 0.1 to 4
- lambda_y: float32 [2048], P('py'), may hold values from 0.1 to 4
- coupling: float32 [9], replicated, may hold values from 0.2 to 2
- layer_shift: float32 [10], replicated, may hold values from 0.05 to 1
- left_x: bfloat16 [2048, 2048], P(None, 'px'), may hold values from -0.125 to 0.125
- left_y: bfloat16 [2048, 2048], P('py'), may hold values from -0.125 to 0.125
- right_y: bfloat16 [2048, 2048], P('py'), may hold values from -0.125 to 0.125
- right_x: bfloat16 [2048, 2048], P(None, 'px'), may hold values from -0.125 to 0.125
- regime_code: int32 [10, 2048, 2048], P(None, 'py', 'px'), may hold values from 0 to 3
- upwind_flag: int32 [2, 10, 2048, 2048], P(None, None, 'py', 'px'), may hold values from 0 to 1
- mobility_table: float32 [4], replicated, may hold values from 0.3 to 3
Outputs:
- correction: float32 [10, 2048, 2048], P(None, 'py', 'px')
- balance: float32 [10, 2048, 2048], P(None, 'py', 'px')
Inputs may be any that keep to these rules, and one draw needn't show every extreme that they name: `regime_code`: a regime number of each cell.
All inputs are finite; a program needn't handle non-finite values.
Results may differ from a plain program's by a relative error of at most 0.0057.
Values may be sent and summed in bfloat16 or wider, within the bound.
No kernel may reach another device: no remote copies, remote signals or barrier semaphores. Data moves between devices by JAX's collectives and lax.ppermute only.
A program may use at most 192 MiB of HBM per device.

v0:
```python
import jax
import jax.numpy as jnp
from jax import lax
from jax.sharding import PartitionSpec as P


def with_halo(block, sides, width):
    for axis, dim in sides:
        count = lax.axis_size(axis)
        forward = [(i, i + 1) for i in range(count - 1)]
        backward = [(target, source) for source, target in forward]
        low = lax.ppermute(
            lax.slice_in_dim(block, block.shape[dim] - width, None, axis=dim), axis, forward
        )
        high = lax.ppermute(lax.slice_in_dim(block, 0, width, axis=dim), axis, backward)
        block = jnp.concatenate([low, block, high], axis=dim)
    return block


def thomas_solve(rhs, lambda_x, lambda_y, coupling, layer_shift):
    layers = rhs.shape[0]
    mode_sum = lambda_y[:, None] + lambda_x[None, :]
    ratios = []
    partial_values = []
    for layer_index in range(layers):
        diagonal = mode_sum + layer_shift[layer_index]
        if layer_index > 0:
            diagonal = diagonal + coupling[layer_index - 1]
        if layer_index < layers - 1:
            diagonal = diagonal + coupling[layer_index]
        if layer_index == 0:
            pivots = diagonal
            solved = rhs[0] / pivots
        else:
            pivots = diagonal + coupling[layer_index - 1] * ratios[-1]
            solved = (rhs[layer_index] + coupling[layer_index - 1] * partial_values[-1]) / pivots
        partial_values.append(solved)
        if layer_index < layers - 1:
            ratios.append(-coupling[layer_index] / pivots)
    results = [partial_values[layers - 1]]
    for layer_index in range(layers - 2, -1, -1):
        results.append(partial_values[layer_index] - ratios[layer_index] * results[-1])
    return jnp.stack(results[::-1])


def shards(
    residual,
    lambda_x,
    lambda_y,
    coupling,
    layer_shift,
    left_x,
    left_y,
    right_y,
    right_x,
    regime_code,
    upwind_flag,
    mobility_table,
):
    rounded = residual.astype(jnp.bfloat16)

    def forward(block):
        weights = left_x
        spectral_x = jnp.einsum(
            "zyx,xi->zyi",
            lax.all_gather(block, "px", axis=2, tiled=True),
            weights,
            preferred_element_type=jnp.float32,
        ).astype(jnp.bfloat16)
        weights = left_y
        return jnp.einsum(
            "jy,zyi->zji",
            weights,
            lax.all_gather(spectral_x, "py", axis=1, tiled=True),
            preferred_element_type=jnp.float32,
        )

    mobility = jnp.zeros(regime_code.shape, jnp.float32)
    for regime in range(mobility_table.shape[0]):
        mobility = jnp.where(regime_code == regime, mobility_table[regime], mobility)
    spectral = forward(rounded)
    solved = thomas_solve(spectral, lambda_x, lambda_y, coupling, layer_shift).astype(jnp.bfloat16)
    weights = right_y
    back_y = jnp.einsum(
        "yj,zji->zyi",
        weights,
        lax.all_gather(solved, "py", axis=1, tiled=True),
        preferred_element_type=jnp.float32,
    ).astype(jnp.bfloat16)
    weights = right_x
    correction = jnp.einsum(
        "zyi,ix->zyx",
        lax.all_gather(back_y, "px", axis=2, tiled=True),
        weights,
        preferred_element_type=jnp.float32,
    )
    width_x = correction.shape[2]
    width_y = correction.shape[1]
    stacked = jnp.stack(
        [
            correction,
            mobility,
            upwind_flag[0].astype(jnp.float32),
            upwind_flag[1].astype(jnp.float32),
        ]
    )
    extended = with_halo(stacked, (("px", 3), ("py", 2)), 1)
    press_x = extended[0][:, 1:-1, :]
    mobil_x = extended[1][:, 1:-1, :]
    flags_x = extended[2][:, 1:-1, :]
    upwind_x = jnp.where(flags_x[:, :, :-1] > 0.5, mobil_x[:, :, :-1], mobil_x[:, :, 1:])
    flux_x = upwind_x * (press_x[:, :, :-1] - press_x[:, :, 1:])
    faces_x = lax.axis_index("px") * width_x + jnp.arange(width_x + 1, dtype=jnp.int32)
    valid_x = (faces_x >= 1) & (faces_x <= width_x * lax.axis_size("px") - 1)
    flux_x = jnp.where(valid_x[None, None, :], flux_x, 0.0)
    net_x = flux_x[:, :, 1:] - flux_x[:, :, :-1]
    press_y = extended[0][:, :, 1:-1]
    mobil_y = extended[1][:, :, 1:-1]
    flags_y = extended[3][:, :, 1:-1]
    upwind_y = jnp.where(flags_y[:, :-1, :] > 0.5, mobil_y[:, :-1, :], mobil_y[:, 1:, :])
    flux_y = upwind_y * (press_y[:, :-1, :] - press_y[:, 1:, :])
    faces_y = lax.axis_index("py") * width_y + jnp.arange(width_y + 1, dtype=jnp.int32)
    valid_y = (faces_y >= 1) & (faces_y <= width_y * lax.axis_size("py") - 1)
    flux_y = jnp.where(valid_y[None, :, None], flux_y, 0.0)
    net_y = flux_y[:, 1:, :] - flux_y[:, :-1, :]
    balance = net_x + net_y
    return (correction, balance)


def solution(mesh):
    return jax.shard_map(
        shards,
        mesh=mesh,
        in_specs=(
            P(None, "py", "px"),
            P("px"),
            P("py"),
            P(),
            P(),
            P(None, "px"),
            P("py", None),
            P("py", None),
            P(None, "px"),
            P(None, "py", "px"),
            P(None, None, "py", "px"),
            P(),
        ),
        out_specs=(P(None, "py", "px"), P(None, "py", "px")),
        check_vma=False,
    )
```

profile of v0, /device:TPU:3, one launch (start us, length us, event | category | flops | bytes accessed | tf_op | source)
XLA Modules:
  0.0 841.1 jit_solution(6633718282841774213)
XLA Ops:
  7.2 4.5 convert_element_type.21
  11.8 106.2 %all-gather.5.cloned.1.call-done = bf16[10,256,2048]{2,1,0:T(8,128)(2,1)} async-done(((bf16[10,256,512]{2,1,0:T(8,128)(2,1)}), bf16[10,256,2048]{2,1,0:T(8,128)(2,1)}) %all-gather.5.cloned.1.call-update) | async-done | bytes 10485776 | tf_op jit(solution)/shard_map/all_gather | solution.py:66
  118.0 9.4 %fusion.9 = bf16[10,256,512]{1,2,0:T(8,128)(2,1)} fusion(bf16[10,256,2048]{2,1,0:T(8,128)(2,1)} %all-gather.5.cloned.1.call-done, bf16[2048,512]{1,0:T(8,128)(2,1)S(1)} %copy-done), kind=kOutput, calls=%fused_computation.41 | convolution fusion | flops 5370019840 | bytes 15204352 | tf_op jit(solution)/shard_map/zyx,xi->zyi/dot_general | solution.py:64
  134.9 179.7 %all-gather.7.cloned.1.call-done = bf16[10,2048,512]{1,2,0:T(8,128)(2,1)} async-done(((bf16[10,256,512]{1,2,0:T(8,128)(2,1)}), bf16[10,2048,512]{1,2,0:T(8,128)(2,1)}) %all-gather.7.cloned.1.call-update) | async-done | bytes 20971536 | tf_op jit(solution)/shard_map/all_gather | solution.py:74
  314.6 10.3 %convolution_bitcast_fusion = f32[10,256,512]{1,2,0:T(8,128)S(1)} fusion(bf16[10,2048,512]{1,2,0:T(8,128)(2,1)} %all-gather.7.cloned.1.call-done, bf16[256,2048]{1,0:T(8,128)(2,1)S(1)} %copy-done.16), kind=kOutput, calls=%fused_computation.36 | convolution fusion | flops 5368709120 | bytes 27262976 | tf_op jit(solution)/shard_map/jy,zyi->zji/dot_general | solution.py:71
  324.9 14.8 %fusion.59 = (bf16[10,256,512]{1,2,0:T(8,128)(2,1)}, bf16[1,256,512]{1,2,0:T(8,128)(2,1)S(1)}, f32[1,256,512]{1,2,0:T(8,128)S(1)}, f32[1,256,512]{1,2,0:T(8,128)...) fusion(f32[]{:T(128)S(6)} %neg.27, f32[]{:T(128)} %bitcast.4, ...), kind=kLoop, calls=%fused_computation.107 | loop fusion | flops 13631487 | bytes 8916080
  340.4 4.8 convert_dynamic-update-slice_fusion.7
  345.9 7.5 convert_dynamic-update-slice_fusion.5
  354.1 10.2 %convert_dynamic-update-slice_fusion.3 = bf16[10,256,512]{1,2,0:T(8,128)(2,1)} fusion(bf16[10,256,512]{1,2,0:T(8,128)(2,1)} %convert_dynamic-update-slice_fusion.4, f32[1,256,512]{1,2,0:T(8,128)S(1)} %get-tuple-element.7, f32[1,256,512]{1,2,0:T(8,128)S(1)} %get-tuple-element.6, f32[]{:T(128)} %bitcast.3, f32[]{:T(128)S(6)} %neg.27, f32[]{:T(128)} %bitcast.4, ...), kind=kLoop, calls=%fused_computation.111 | loop fusion | flops 5636096 | bytes 1320988
  365.1 13.9 %convert_dynamic-update-slice_fusion.1 = bf16[10,256,512]{1,2,0:T(8,128)(2,1)} fusion(bf16[10,256,512]{1,2,0:T(8,128)(2,1)} %convert_dynamic-update-slice_fusion.2, f32[]{:T(128)} %bitcast.3, f32[]{:T(128)S(6)} %neg.27, f32[]{:T(128)} %bitcast.4, f32[]{:T(128)} %bitcast.5, f32[]{:T(128)S(6)} %neg.28, f32[]{:T(128)} %bitcast.6, f32[]{:T(128)} %bitcast.7, ...), kind=kLoop, calls=%fused_computation.109 | loop fusion | flops 8912896 | bytes 2372132
  379.0 13.9 %convert_dynamic-update-slice_fusion = bf16[10,256,512]{1,2,0:T(8,128)(2,1)} fusion(bf16[10,256,512]{1,2,0:T(8,128)(2,1)} %convert_dynamic-update-slice_fusion.1, f32[]{:T(128)} %bitcast.3, f32[]{:T(128)S(6)} %neg.27, f32[]{:T(128)} %bitcast.4, f32[]{:T(128)} %bitcast.5, f32[]{:T(128)S(6)} %neg.28, f32[]{:T(128)} %bitcast.6, f32[]{:T(128)} %bitcast.7, ...), kind=kLoop, calls=%fused_computation.108 | loop fusion | flops 8650752 | bytes 2372132 | tf_op jit(solution)/shard_map/stack | solution.py:43
  393.1 184.6 %all-gather.9.cloned.1.call-done = bf16[10,2048,512]{1,2,0:T(8,128)(2,1)} async-done(((bf16[10,256,512]{1,2,0:T(8,128)(2,1)}), bf16[10,2048,512]{1,2,0:T(8,128)(2,1)}) %all-gather.9.cloned.1.call-update) | async-done | bytes 20971536 | tf_op jit(solution)/shard_map/all_gather | solution.py:87
  577.7 22.0 %convert_bitcast_fusion = bf16[10,256,512]{2,1,0:T(8,128)(2,1)} fusion(bf16[10,2048,512]{1,2,0:T(8,128)(2,1)} %all-gather.9.cloned.1.call-done, bf16[256,2048]{1,0:T(8,128)(2,1)S(1)} %copy-done.17), kind=kOutput, calls=%fused_computation.25 | convolution fusion | flops 5370019840 | bytes 24641536 | tf_op jit(solution)/shard_map/yj,zji->zyi/dot_general | solution.py:84
  600.5 9.1 %select_bitcast_fusion = f32[1,10,256,512]{3,2,1,0:T(8,128)} fusion(s32[10,256,512]{2,1,0:T(8,128)} %param.21, f32[]{:T(128)} %bitcast.29, f32[]{:T(128)} %bitcast.28, f32[]{:T(128)} %bitcast.27, f32[]{:T(128)} %bitcast.26), kind=kLoop, calls=%fused_computation.24 | loop fusion | flops 10485760 | bytes 10485776 | tf_op jit(solution)/shard_map/stack | solution.py:99
  609.6 10.4 %slice_convert_fusion.1 = (f32[1,10,256,512]{3,2,1,0:T(8,128)}, f32[1,10,256,512]{3,2,1,0:T(8,128)}) fusion(s32[2,10,256,512]{3,2,1,0:T(8,128)} %param.22), kind=kLoop, calls=%fused_computation.23 | loop fusion | flops 2621440 | bytes 20971520 | tf_op jit(solution)/shard_map/convert_element_type | solution.py:103
  620.0 82.6 %all-gather.11.cloned.1.call-done = bf16[10,256,2048]{2,1,0:T(8,128)(2,1)} async-done(((bf16[10,256,512]{2,1,0:T(8,128)(2,1)}), bf16[10,256,2048]{2,1,0:T(8,128)(2,1)}) %all-gather.11.cloned.1.call-update) | async-done | bytes 10485776 | tf_op jit(solution)/shard_map/all_gather | solution.py:93
  702.6 8.5 %fusion.5 = f32[10,256,512]{2,1,0:T(8,128)S(1)} fusion(bf16[10,256,2048]{2,1,0:T(8,128)(2,1)} %all-gather.11.cloned.1.call-done, bf16[2048,512]{1,0:T(8,128)(2,1)S(1)} %copy-done.15), kind=kOutput, calls=%fused_computation.37 | convolution fusion | flops 5368709120 | bytes 17825792 | tf_op jit(solution)/shard_map/zyi,ix->zyx/dot_general | solution.py:91
  711.2 5.9 pad_maximum_fusion.4
  737.9 5.4 collective-permute-start.2
  749.3 27.6 %pad_maximum_fusion = f32[4,10,258,514]{3,2,1,0:T(8,128)} fusion(f32[4,10,1,514]{3,2,1,0:T(1,128)S(1)} %collective-permute-done.3, f32[4,10,256,1]{3,2,1,0:T(8,128)S(1)} %copy-done.8, f32[1,10,256,512]{3,2,1,0:T(8,128)} %get-tuple-element.19, f32[1,10,256,512]{3,2,1,0:T(8,128)S(1)} %bitcast.57, f32[1,10,256,512]{3,2,1,0:T(8,128)} %select_bitcast_fusion, ...), kind=kLoop, calls=%fused_computation | loop fusion | flops 37131360 | bytes 42435840 | tf_op jit(solution)/shard_map/concatenate | solution.py:16
  776.9 18.6 %slice_bitcast_fusion.3 = (f32[10,258,514]{2,1,0:T(8,128)}, f32[10,258,514]{2,1,0:T(8,128)}, f32[10,258,514]{2,1,0:T(8,128)}, f32[10,258,514]{2,1,0:T(8,128)}) fusion(f32[4,10,258,514]{3,2,1,0:T(8,128)} %pad_maximum_fusion), kind=kLoop, calls=%fused_computation.4 | loop fusion | bytes 42435840 | tf_op jit(solution)/shard_map/squeeze | solution.py:110
  795.5 14.9 %fusion.1 = f32[10,256,513]{2,1,0:T(8,128)} fusion(f32[10,258,514]{2,1,0:T(8,128)} %get-tuple-element.14, f32[10,258,514]{2,1,0:T(8,128)} %get-tuple-element.15, f32[10,258,514]{2,1,0:T(8,128)} %get-tuple-element.12, pred[513]{0:T(1024)(128)(4,1)S(1)} %fusion.62), kind=kLoop, calls=%fused_computation.7 | loop fusion | flops 6566400 | bytes 31519232 | tf_op jit(solution)/shard_map/jit(_where)/select_n | solution.py:115
  812.3 10.7 %fusion.3 = f32[10,257,512]{2,1,0:T(8,128)} fusion(f32[10,258,514]{2,1,0:T(8,128)S(1)} %copy-done.2, f32[10,258,514]{2,1,0:T(8,128)S(1)} %copy-done.3, f32[10,258,514]{2,1,0:T(8,128)} %get-tuple-element.13, pred[257]{0:T(512)(128)(4,1)S(1)} %fusion.65), kind=kLoop, calls=%fused_computation.12 | loop fusion | flops 6579200 | bytes 31580416 | tf_op jit(solution)/shard_map/jit(_where)/select_n | solution.py:124
  823.1 11.2 %fusion.4 = f32[10,256,512]{2,1,0:T(8,128)} fusion(f32[10,257,512]{2,1,0:T(8,128)} %fusion.3, f32[10,256,513]{2,1,0:T(8,128)} %fusion.1), kind=kLoop, calls=%fused_computation.16 | loop fusion | flops 3932160 | bytes 26214400 | tf_op jit(solution)/shard_map/add | solution.py:126
  (70 shorter events, 34.6 us)
Async XLA Ops:
  7.2 110.8 %copy-start = (bf16[2048,512]{1,0:T(8,128)(2,1)S(1)}, bf16[2048,512]{1,0:T(8,128)(2,1)}, u32[]{:S(2)}) copy-start(bf16[2048,512]{1,0:T(8,128)(2,1)} %param.17) | copy-start | bytes 6291460
  7.2 110.8 %all-gather.5.cloned.1.call-start = ((), (), s32[]{:S(2)}) async-start(), calls=%async_computation | async-start | bytes 13107200 | tf_op jit(solution)/shard_map/all_gather | solution.py:66
  11.7 116.3 %copy-start.12 = (f32[9]{0:T(128)S(1)}, f32[9]{0:T(128)}, u32[]{:S(2)}) copy-start(f32[9]{0:T(128)} %param.15) | copy-start | bytes 112
  11.7 122.4 %copy-start.11 = (f32[10]{0:T(128)S(1)}, f32[10]{0:T(128)}, u32[]{:S(2)}) copy-start(f32[10]{0:T(128)} %param.16) | copy-start | bytes 124
  11.8 302.8 %copy-start.16 = (bf16[256,2048]{1,0:T(8,128)(2,1)S(1)}, bf16[256,2048]{1,0:T(8,128)(2,1)}, u32[]{:S(2)}) copy-start(bf16[256,2048]{1,0:T(8,128)(2,1)} %param.18) | copy-start | bytes 3145732
  11.8 302.8 %all-gather.7.cloned.1.call-start = ((), (), s32[]{:S(2)}) async-start(), calls=%async_computation.1 | async-start | bytes 23592960 | tf_op jit(solution)/shard_map/all_gather | solution.py:74
  127.5 450.3 %all-gather.9.cloned.1.call-start = ((), (), s32[]{:S(2)}) async-start(), calls=%async_computation.2 | async-start | bytes 23592960 | tf_op jit(solution)/shard_map/all_gather | solution.py:87
  134.9 190.0 %copy-start.10 = (f32[512]{0:T(512)S(1)}, f32[512]{0:T(512)}, u32[]{:S(2)}) copy-start(f32[512]{0:T(512)} %param.13) | copy-start | bytes 6148
  134.9 190.0 %copy-start.13 = (f32[256]{0:T(256)S(1)}, f32[256]{0:T(256)}, u32[]{:S(2)}) copy-start(f32[256]{0:T(256)} %param.14) | copy-start | bytes 3076
  353.4 224.4 %copy-start.17 = (bf16[256,2048]{1,0:T(8,128)(2,1)S(1)}, bf16[256,2048]{1,0:T(8,128)(2,1)}, u32[]{:S(2)}) copy-start(bf16[256,2048]{1,0:T(8,128)(2,1)} %param.19) | copy-start | bytes 3145732
  392.9 206.9 %copy-start.14 = (f32[4]{0:T(128)S(1)}, f32[4]{0:T(128)}, u32[]{:S(2)}) copy-start(f32[4]{0:T(128)} %param.23) | copy-start | bytes 52
  392.9 309.7 %all-gather.11.cloned.1.call-start = ((), (), s32[]{:S(2)}) async-start(), calls=%async_computation.3 | async-start | bytes 13107200 | tf_op jit(solution)/shard_map/all_gather | solution.py:93
  609.6 93.0 %copy-start.15 = (bf16[2048,512]{1,0:T(8,128)(2,1)S(1)}, bf16[2048,512]{1,0:T(8,128)(2,1)}, u32[]{:S(2)}) copy-start(bf16[2048,512]{1,0:T(8,128)(2,1)} %param.20) | copy-start | bytes 6291460
  720.4 8.6 %collective-permute-start = (f32[4,10,256,1]{2,0,3,1:T(4,128)S(1)}, f32[4,10,256,1]{2,0,3,1:T(4,128)S(1)}, u32[]{:S(2)}, u32[]{:S(2)}) collective-permute-start(f32[4,10,256,1]{2,0,3,1:T(4,128)S(1)} %copy.14), channel_id=1, source_target_pairs={{0,8},{8,16},{16,24},{1,9},{9,17},{17,25},{2,10},{10,18},{18,26},{... | collective-permute-start | bytes 122888 | tf_op jit(solution)/shard_map/ppermute | solution.py:12
  726.8 5.6 collective-permute-start.1
  732.5 16.8 %slice-start = ((s8[5242880]{0:T(1024)(128)(4,1)}), s8[1048576]{0:T(1024)(128)(4,1)S(1)}, s32[]{:S(2)}) async-start(s8[5242880]{0:T(1024)(128)(4,1)} %bitcast.56), calls=%async_computation.4 | async-start | bytes 2097152
  735.6 13.7 %slice-start.1 = ((s8[5242880]{0:T(1024)(128)(4,1)}), s8[4194304]{0:T(1024)(128)(4,1)S(1)}, s32[]{:S(2)}) async-start(s8[5242880]{0:T(1024)(128)(4,1)} %bitcast.56), calls=%async_computation.5 | async-start | bytes 8388608
  735.6 13.7 %copy-start.7 = (f32[4,10,256,1]{3,2,1,0:T(8,128)S(1)}, f32[4,10,256,1]{3,2,1,0:T(8,128)}, u32[]{:S(2)}) copy-start(f32[4,10,256,1]{3,2,1,0:T(8,128)} %copy.16) | copy-start | bytes 122884
  735.6 13.7 %copy-start.8 = (f32[4,10,256,1]{3,2,1,0:T(8,128)S(1)}, f32[4,10,256,1]{3,2,1,0:T(8,128)}, u32[]{:S(2)}) copy-start(f32[4,10,256,1]{3,2,1,0:T(8,128)} %copy.17) | copy-start | bytes 122884
  737.9 7.5 collective-permute-start.2
  743.3 6.0 collective-permute-start.3
  795.5 14.9 %copy-start.2 = (f32[10,258,514]{2,1,0:T(8,128)S(1)}, f32[10,258,514]{2,1,0:T(8,128)}, u32[]{:S(2)}) copy-start(f32[10,258,514]{2,1,0:T(8,128)} %get-tuple-element.14) | copy-start | bytes 15913444
  795.5 16.9 %copy-start.3 = (f32[10,258,514]{2,1,0:T(8,128)S(1)}, f32[10,258,514]{2,1,0:T(8,128)}, u32[]{:S(2)}) copy-start(f32[10,258,514]{2,1,0:T(8,128)} %get-tuple-element.15) | copy-start | bytes 15913444
  823.1 11.2 %copy-start.1 = (bf16[2048,512]{1,0:T(8,128)(2,1)S(1)}, bf16[2048,512]{1,0:T(8,128)(2,1)}, u32[]{:S(2)}) copy-start(bf16[2048,512]{1,0:T(8,128)(2,1)} %param.17) | copy-start | bytes 6291460
  (4 other events, 31.6 us)
Sparse Core Ops, SparseCore 0:
  11.9 106.1 all-gather.4
  127.6 186.9 all-gather.6
  393.0 184.6 all-gather.8
  599.9 102.6 all-gather.10
where the time goes:
time: 845 us; the launch traced here: 841 us
  waiting for transfers between devices  557 us (66%)
  other arithmetic  164 us (19%)
  matrix products  50.2 us (6%)
  local copies, waits for them, and re-layouts  36.2 us (4%)
  between operations  19.7 us (2%)
  starting transfers between devices  13.6 us (2%)
    all_gather x1, waiting for transfers between devices, shards(): lax.all_gather(solved, 'py', axis=1, tiled=True)  185 us
    all_gather x1, waiting for transfers between devices, forward(): lax.all_gather(spectral_x, 'py', axis=1, tiled=True)  180 us
    all_gather x1, waiting for transfers between devices, forward(): lax.all_gather(block, 'px', axis=2, tiled=True)  106 us
    all_gather x1, waiting for transfers between devices, shards(): lax.all_gather(back_y, 'px', axis=2, tiled=True)  82.6 us
    unnamed x9, other arithmetic  53.4 us
    concatenate x1, other arithmetic, with_halo(): block = jnp.concatenate([low, block, high], axis=dim)  27.6 us
    dot_general x1, matrix products, shards(): jnp.einsum('yj,zji->zyi', weights, lax.all_gather(solved, 'py', axis=1, t...  22 us
    squeeze x1, local copies, waits for them, and re-layouts, shards(): flags_x = extended[2][:, 1:-1, :]  18.6 us
  transfers between devices with their start and end apart: 8, of which 6 were waited for; matrix products, arithmetic and copies ran while one was open for 3% of the time, Pallas kernels for 0%

commit v1 on v0

--- a/solution.py
+++ b/solution.py
@@ -1,7 +1,38 @@
+import functools
 import jax
 import jax.numpy as jnp
 from jax import lax
 from jax.sharding import PartitionSpec as P
+
+
+def mix_slabs(field_in, shard_axis, join_dim):
+    parts_out = lax.axis_index(shard_axis)
+    last = lax.axis_size(shard_axis)
+    part_now, top, then = (last, parts_out, field_in.shape[join_dim])
+    ledger = [
+        to_i * part_now if nth == join_dim else to_i for nth, to_i in enumerate(field_in.shape)
+    ]
+    piece_now = jnp.zeros(ledger, field_in.dtype)
+    main = lax.dynamic_update_slice_in_dim(piece_now, field_in, top * then, axis=join_dim)
+    e_next = row_out = field_in
+    for h in range(1, part_now // 2 + 1):
+        e_next = lax.ppermute(
+            e_next, shard_axis, [(nth, (nth + 1) % part_now) for nth in range(part_now)]
+        )
+        main = lax.dynamic_update_slice_in_dim(
+            main, e_next, (top - h) % part_now * then, axis=join_dim
+        )
+        if 2 * h < part_now:
+            row_out = lax.ppermute(
+                row_out, shard_axis, [(nth, (nth - 1) % part_now) for nth in range(part_now)]
+            )
+            main = lax.dynamic_update_slice_in_dim(
+                main, row_out, (top + h) % part_now * then, axis=join_dim
+            )
+    return main
+
+
+roads_change = functools.partial(mix_slabs, shard_axis="px", join_dim=2)
 
 
 def with_halo(block, sides, width):
@@ -89,10 +120,7 @@
     ).astype(jnp.bfloat16)
     weights = right_x
     correction = jnp.einsum(
-        "zyi,ix->zyx",
-        lax.all_gather(back_y, "px", axis=2, tiled=True),
-        weights,
-        preferred_element_type=jnp.float32,
+        "zyi,ix->zyx", roads_change(back_y), weights, preferred_element_type=jnp.float32
     )
     width_x = correction.shape[2]
     width_y = correction.shape[1]

time: 845 us -> 913 us (1.080)
  waiting for transfers between devices: 557 us -> 596 us
  local copies, waits for them, and re-layouts: 36.2 us -> 70.2 us
  matrix products: 50.2 us -> 41 us
    ppermute x0 -> x3, waiting for transfers between devices: none -> 122 us  [the longest x2 102 us: mix_slabs(): lax.ppermute(e_next, shard_axis, [(nth, (nth + 1) % part_now) for nth in...]
    all_gather x1 -> x0, waiting for transfers between devices: 82.6 us -> none  [shards(): lax.all_gather(back_y, 'px', axis=2, tiled=True)]
    ppermute x0 -> x3, local copies, waits for them, and re-layouts: none -> 13.2 us  [the longest x2 8.8 us: mix_slabs(): lax.ppermute(e_next, shard_axis, [(nth, (nth + 1) % part_now) for nth in...]
    dynamic_update_slice x0 -> x4, local copies, waits for them, and re-layouts: none -> 11 us  [the longest x2 7.39 us: mix_slabs(): lax.dynamic_update_slice_in_dim(main, e_next, (top - h) % part_now * then...]
    dot_general x1, matrix products: 22 us -> 12.1 us  [shards(): jnp.einsum('yj,zji->zyi', weights, lax.all_gather(solved, 'py', axis=1, t...]
    unnamed x9 -> x12, other arithmetic: 53.4 us -> 54.1 us
  transfers between devices with their start and end apart: 8 -> 10, of which waited for: 6 -> 8; matrix products, arithmetic and copies ran while one was open for 3% -> 6% of each run, Pallas kernels for 0% -> 0%
where the time goes in v1:
time: 913 us; the launch traced here: 908 us
  waiting for transfers between devices  596 us (65%)
  other arithmetic  164 us (18%)
  local copies, waits for them, and re-layouts  70.2 us (8%)
  matrix products  41 us (4%)
  between operations  20 us (2%)
  starting transfers between devices  16.1 us (2%)
    all_gather x1, waiting for transfers between devices, shards(): lax.all_gather(solved, 'py', axis=1, tiled=True)  185 us
    all_gather x1, waiting for transfers between devices, forward(): lax.all_gather(spectral_x, 'py', axis=1, tiled=True)  180 us
    all_gather x1, waiting for transfers between devices, forward(): lax.all_gather(block, 'px', axis=2, tiled=True)  106 us
    ppermute x2, waiting for transfers between devices, mix_slabs(): lax.ppermute(e_next, shard_axis, [(nth, (nth + 1) % part_now) for nth in...  102 us
    unnamed x12, other arithmetic  54.1 us
    concatenate x1, other arithmetic, with_halo(): block = jnp.concatenate([low, block, high], axis=dim)  27.8 us
    ppermute x1, waiting for transfers between devices, mix_slabs(): lax.ppermute(row_out, shard_axis, [(nth, (nth - 1) % part_now) for nth in...  19.6 us
    squeeze x1, local copies, waits for them, and re-layouts, shards(): flags_x = extended[2][:, 1:-1, :]  18.6 us
  transfers between devices with their start and end apart: 10, of which 8 were waited for; matrix products, arithmetic and copies ran while one was open for 6% of the time, Pallas kernels for 0%

profile of v1, /device:TPU:3, one launch (start us, length us, event | category | flops | bytes accessed | tf_op | source)
XLA Modules:
  0.0 907.7 jit_solution(17692682190680909840)
XLA Ops:
  11.8 106.2 %all-gather.4.cloned.1.call-done = bf16[10,256,2048]{2,1,0:T(8,128)(2,1)} async-done(((bf16[10,256,512]{2,1,0:T(8,128)(2,1)}), bf16[10,256,2048]{2,1,0:T(8,128)(2,1)}) %all-gather.4.cloned.1.call-update) | async-done | bytes 10485776 | tf_op jit(solution)/shard_map/all_gather | solution.py:97
  118.0 9.4 %fusion.9 = bf16[10,256,512]{1,2,0:T(8,128)(2,1)} fusion(bf16[10,256,2048]{2,1,0:T(8,128)(2,1)} %all-gather.4.cloned.1.call-done, bf16[2048,512]{1,0:T(8,128)(2,1)S(1)} %copy-done), kind=kOutput, calls=%fused_computation.41 | convolution fusion | flops 5370019840 | bytes 15204352 | tf_op jit(solution)/shard_map/zyx,xi->zyi/dot_general | solution.py:95
  134.9 179.7 %all-gather.6.cloned.1.call-done = bf16[10,2048,512]{1,2,0:T(8,128)(2,1)} async-done(((bf16[10,256,512]{1,2,0:T(8,128)(2,1)}), bf16[10,2048,512]{1,2,0:T(8,128)(2,1)}) %all-gather.6.cloned.1.call-update) | async-done | bytes 20971536 | tf_op jit(solution)/shard_map/all_gather | solution.py:105
  314.6 10.3 %convolution_bitcast_fusion = f32[10,256,512]{1,2,0:T(8,128)S(1)} fusion(bf16[10,2048,512]{1,2,0:T(8,128)(2,1)} %all-gather.6.cloned.1.call-done, bf16[256,2048]{1,0:T(8,128)(2,1)S(1)} %copy-done.15), kind=kOutput, calls=%fused_computation.36 | convolution fusion | flops 5368709120 | bytes 27262976 | tf_op jit(solution)/shard_map/jy,zyi->zji/dot_general | solution.py:102
  324.9 14.9 %fusion.59 = (bf16[10,256,512]{1,2,0:T(8,128)(2,1)}, bf16[1,256,512]{1,2,0:T(8,128)(2,1)S(1)}, f32[1,256,512]{1,2,0:T(8,128)S(1)}, f32[1,256,512]{1,2,0:T(8,128)...) fusion(f32[]{:T(128)S(6)} %neg.27, f32[]{:T(128)} %bitcast.4, ...), kind=kLoop, calls=%fused_computation.107 | loop fusion | flops 13631487 | bytes 8916080
  346.2 7.7 convert_dynamic-update-slice_fusion.5
  354.6 10.4 %convert_dynamic-update-slice_fusion.3 = bf16[10,256,512]{1,2,0:T(8,128)(2,1)} fusion(bf16[10,256,512]{1,2,0:T(8,128)(2,1)} %convert_dynamic-update-slice_fusion.4, f32[1,256,512]{1,2,0:T(8,128)S(1)} %get-tuple-element.7, f32[1,256,512]{1,2,0:T(8,128)S(1)} %get-tuple-element.6, f32[]{:T(128)} %bitcast.3, f32[]{:T(128)S(6)} %neg.27, f32[]{:T(128)} %bitcast.4, ...), kind=kLoop, calls=%fused_computation.111 | loop fusion | flops 5636096 | bytes 1320988
  365.7 14.0 %convert_dynamic-update-slice_fusion.1 = bf16[10,256,512]{1,2,0:T(8,128)(2,1)} fusion(bf16[10,256,512]{1,2,0:T(8,128)(2,1)} %convert_dynamic-update-slice_fusion.2, f32[]{:T(128)} %bitcast.3, f32[]{:T(128)S(6)} %neg.27, f32[]{:T(128)} %bitcast.4, f32[]{:T(128)} %bitcast.5, f32[]{:T(128)S(6)} %neg.28, f32[]{:T(128)} %bitcast.6, f32[]{:T(128)} %bitcast.7, ...), kind=kLoop, calls=%fused_computation.109 | loop fusion | flops 8912896 | bytes 2372132
  379.7 14.0 %convert_dynamic-update-slice_fusion = bf16[10,256,512]{1,2,0:T(8,128)(2,1)} fusion(bf16[10,256,512]{1,2,0:T(8,128)(2,1)} %convert_dynamic-update-slice_fusion.1, f32[]{:T(128)} %bitcast.3, f32[]{:T(128)S(6)} %neg.27, f32[]{:T(128)} %bitcast.4, f32[]{:T(128)} %bitcast.5, f32[]{:T(128)S(6)} %neg.28, f32[]{:T(128)} %bitcast.6, f32[]{:T(128)} %bitcast.7, ...), kind=kLoop, calls=%fused_computation.108 | loop fusion | flops 8650752 | bytes 2372132 | tf_op jit(solution)/shard_map/stack | solution.py:74
  393.8 184.8 %all-gather.8.cloned.1.call-done = bf16[10,2048,512]{1,2,0:T(8,128)(2,1)} async-done(((bf16[10,256,512]{1,2,0:T(8,128)(2,1)}), bf16[10,2048,512]{1,2,0:T(8,128)(2,1)}) %all-gather.8.cloned.1.call-update) | async-done | bytes 20971536 | tf_op jit(solution)/shard_map/all_gather | solution.py:118
  578.6 12.1 %convert_bitcast_fusion = bf16[10,256,512]{1,2,0:T(8,128)(2,1)} fusion(bf16[10,2048,512]{1,2,0:T(8,128)(2,1)} %all-gather.8.cloned.1.call-done, bf16[256,2048]{1,0:T(8,128)(2,1)S(1)} %copy-done.16), kind=kOutput, calls=%fused_computation.25 | convolution fusion | flops 5370019840 | bytes 24641536 | tf_op jit(solution)/shard_map/yj,zji->zyi/dot_general | solution.py:115
  592.2 57.1 %collective-permute-done = bf16[10,256,512]{1,2,0:T(8,128)(2,1)} collective-permute-done((bf16[10,256,512]{1,2,0:T(8,128)(2,1)}, bf16[10,256,512]{1,2,0:T(8,128)(2,1)}, u32[]{:S(2)}, u32[]{:S(2)}) %collective-permute-start) | collective-permute-done | bytes 2621472 | tf_op jit(solution)/shard_map/ppermute | solution.py:19
  652.0 8.6 select_bitcast_fusion
  660.6 9.8 %slice_convert_fusion.1 = (f32[1,10,256,512]{3,2,1,0:T(8,128)}, f32[1,10,256,512]{3,2,1,0:T(8,128)}) fusion(s32[2,10,256,512]{3,2,1,0:T(8,128)} %param.22), kind=kLoop, calls=%fused_computation.23 | loop fusion | flops 2621440 | bytes 20971520 | tf_op jit(solution)/shard_map/convert_element_type | solution.py:131
  675.1 5.4 broadcast_in_dim.47
  686.7 19.6 %collective-permute-done.1 = bf16[10,256,512]{1,2,0:T(8,128)(2,1)} collective-permute-done((bf16[10,256,512]{1,2,0:T(8,128)(2,1)}, bf16[10,256,512]{1,2,0:T(8,128)(2,1)}, u32[]{:S(2)}, u32[]{:S(2)}) %collective-permute-start.1) | collective-permute-done | bytes 2621472 | tf_op jit(solution)/shard_map/ppermute | solution.py:26
  716.2 45.4 %collective-permute-done.2 = bf16[10,256,512]{1,2,0:T(8,128)(2,1)} collective-permute-done((bf16[10,256,512]{1,2,0:T(8,128)(2,1)}, bf16[10,256,512]{1,2,0:T(8,128)(2,1)}, u32[]{:S(2)}, u32[]{:S(2)}) %collective-permute-start.2) | collective-permute-done | bytes 2621472 | tf_op jit(solution)/shard_map/ppermute | solution.py:19
  769.7 9.1 %fusion.5 = f32[10,256,512]{2,1,0:T(8,128)S(1)} fusion(bf16[10,256,2048]{2,1,0:T(8,128)(2,1)} %constant_dynamic-update-slice_fusion, bf16[2048,512]{1,0:T(8,128)(2,1)S(1)} %copy-done.14), kind=kOutput, calls=%fused_computation.37 | convolution fusion | flops 5368709120 | bytes 17825792 | tf_op jit(solution)/shard_map/zyi,ix->zyx/dot_general | solution.py:122
  778.9 5.9 pad_maximum_fusion.4
  815.7 27.8 %pad_maximum_fusion = f32[4,10,258,514]{3,2,1,0:T(8,128)} fusion(f32[4,10,1,514]{3,2,1,0:T(1,128)S(1)} %collective-permute-done.6, f32[4,10,256,1]{3,2,1,0:T(8,128)S(1)} %copy-done.5, f32[1,10,256,512]{3,2,1,0:T(8,128)} %get-tuple-element.19, f32[1,10,256,512]{3,2,1,0:T(8,128)S(1)} %bitcast.59, f32[1,10,256,512]{3,2,1,0:T(8,128)} %select_bitcast_fusion, ...), kind=kLoop, calls=%fused_computation | loop fusion | flops 37131360 | bytes 42435840 | tf_op jit(solution)/shard_map/concatenate | solution.py:47
  843.6 18.6 %slice_bitcast_fusion.3 = (f32[10,258,514]{2,1,0:T(8,128)}, f32[10,258,514]{2,1,0:T(8,128)}, f32[10,258,514]{2,1,0:T(8,128)}, f32[10,258,514]{2,1,0:T(8,128)}) fusion(f32[4,10,258,514]{3,2,1,0:T(8,128)} %pad_maximum_fusion), kind=kLoop, calls=%fused_computation.4 | loop fusion | bytes 42435840 | tf_op jit(solution)/shard_map/squeeze | solution.py:138
  862.1 15.1 %fusion.1 = f32[10,256,513]{2,1,0:T(8,128)} fusion(f32[10,258,514]{2,1,0:T(8,128)} %get-tuple-element.14, f32[10,258,514]{2,1,0:T(8,128)} %get-tuple-element.15, f32[10,258,514]{2,1,0:T(8,128)} %get-tuple-element.12, pred[513]{0:T(1024)(128)(4,1)S(1)} %fusion.62), kind=kLoop, calls=%fused_computation.7 | loop fusion | flops 6566400 | bytes 31519232 | tf_op jit(solution)/shard_map/jit(_where)/select_n | solution.py:143
  879.0 10.7 %fusion.3 = f32[10,257,512]{2,1,0:T(8,128)} fusion(f32[10,258,514]{2,1,0:T(8,128)S(1)} %copy-done.2, f32[10,258,514]{2,1,0:T(8,128)S(1)} %copy-done.3, f32[10,258,514]{2,1,0:T(8,128)} %get-tuple-element.13, pred[257]{0:T(512)(128)(4,1)S(1)} %fusion.65), kind=kLoop, calls=%fused_computation.12 | loop fusion | flops 6579200 | bytes 31580416 | tf_op jit(solution)/shard_map/jit(_where)/select_n | solution.py:152
  889.7 11.2 %fusion.4 = f32[10,256,512]{2,1,0:T(8,128)} fusion(f32[10,257,512]{2,1,0:T(8,128)} %fusion.3, f32[10,256,513]{2,1,0:T(8,128)} %fusion.1), kind=kLoop, calls=%fused_computation.16 | loop fusion | flops 3932160 | bytes 26214400 | tf_op jit(solution)/shard_map/add | solution.py:154
  (95 shorter events, 79.7 us)
Async XLA Ops:
  7.2 110.8 %copy-start = (bf16[2048,512]{1,0:T(8,128)(2,1)S(1)}, bf16[2048,512]{1,0:T(8,128)(2,1)}, u32[]{:S(2)}) copy-start(bf16[2048,512]{1,0:T(8,128)(2,1)} %param.17) | copy-start | bytes 6291460
  7.2 110.8 %all-gather.4.cloned.1.call-start = ((), (), s32[]{:S(2)}) async-start(), calls=%async_computation | async-start | bytes 13107200 | tf_op jit(solution)/shard_map/all_gather | solution.py:97
  11.7 116.1 %copy-start.11 = (f32[9]{0:T(128)S(1)}, f32[9]{0:T(128)}, u32[]{:S(2)}) copy-start(f32[9]{0:T(128)} %param.15) | copy-start | bytes 112
  11.7 122.5 %copy-start.10 = (f32[10]{0:T(128)S(1)}, f32[10]{0:T(128)}, u32[]{:S(2)}) copy-start(f32[10]{0:T(128)} %param.16) | copy-start | bytes 124
  11.8 302.8 %copy-start.15 = (bf16[256,2048]{1,0:T(8,128)(2,1)S(1)}, bf16[256,2048]{1,0:T(8,128)(2,1)}, u32[]{:S(2)}) copy-start(bf16[256,2048]{1,0:T(8,128)(2,1)} %param.18) | copy-start | bytes 3145732
  11.8 302.8 %all-gather.6.cloned.1.call-start = ((), (), s32[]{:S(2)}) async-start(), calls=%async_computation.1 | async-start | bytes 23592960 | tf_op jit(solution)/shard_map/all_gather | solution.py:105
  127.5 451.1 %all-gather.8.cloned.1.call-start = ((), (), s32[]{:S(2)}) async-start(), calls=%async_computation.2 | async-start | bytes 23592960 | tf_op jit(solution)/shard_map/all_gather | solution.py:118
  134.9 190.0 %copy-start.9 = (f32[512]{0:T(512)S(1)}, f32[512]{0:T(512)}, u32[]{:S(2)}) copy-start(f32[512]{0:T(512)} %param.13) | copy-start | bytes 6148
  134.9 190.0 %copy-start.12 = (f32[256]{0:T(256)S(1)}, f32[256]{0:T(256)}, u32[]{:S(2)}) copy-start(f32[256]{0:T(256)} %param.14) | copy-start | bytes 3076
  353.9 224.7 %copy-start.16 = (bf16[256,2048]{1,0:T(8,128)(2,1)S(1)}, bf16[256,2048]{1,0:T(8,128)(2,1)}, u32[]{:S(2)}) copy-start(bf16[256,2048]{1,0:T(8,128)(2,1)} %param.19) | copy-start | bytes 3145732
  393.8 257.6 %copy-start.13 = (f32[4]{0:T(128)S(1)}, f32[4]{0:T(128)}, u32[]{:S(2)}) copy-start(f32[4]{0:T(128)} %param.23) | copy-start | bytes 52
  590.7 58.5 %collective-permute-start = (bf16[10,256,512]{1,2,0:T(8,128)(2,1)}, bf16[10,256,512]{1,2,0:T(8,128)(2,1)}, u32[]{:S(2)}, u32[]{:S(2)}) collective-permute-start(bf16[10,256,512]{1,2,0:T(8,128)(2,1)} %convert_bitcast_fusion), channel_id=1, source_target_pairs={{0,8},{8,16},{16,24},{24,0},{1,9},{9,17},{17,25},{25,1},{2,10},{10... | collective-permute-start | bytes 7864328 | tf_op jit(solution)/shard_map/ppermute | solution.py:19
  591.9 114.4 %collective-permute-start.1 = (bf16[10,256,512]{1,2,0:T(8,128)(2,1)}, bf16[10,256,512]{1,2,0:T(8,128)(2,1)}, u32[]{:S(2)}, u32[]{:S(2)}) collective-permute-start(bf16[10,256,512]{1,2,0:T(8,128)(2,1)} %convert_bitcast_fusion), channel_id=1, source_target_pairs={{0,24},{8,0},{16,8},{24,16},{1,25},{9,1},{17,9},{25,17},{2,26},{10... | collective-permute-start | bytes 7864328 | tf_op jit(solution)/shard_map/ppermute | solution.py:26
  649.3 112.4 %collective-permute-start.2 = (bf16[10,256,512]{1,2,0:T(8,128)(2,1)}, bf16[10,256,512]{1,2,0:T(8,128)(2,1)}, u32[]{:S(2)}, u32[]{:S(2)}) collective-permute-start(bf16[10,256,512]{1,2,0:T(8,128)(2,1)} %collective-permute-done), channel_id=1, source_target_pairs={{0,8},{8,16},{16,24},{24,0},{1,9},{9,17},{17,25},{25,1},{2,10},{10... | collective-permute-start | bytes 7864328 | tf_op jit(solution)/shard_map/ppermute | solution.py:19
  716.2 53.5 %copy-start.14 = (bf16[2048,512]{1,0:T(8,128)(2,1)S(1)}, bf16[2048,512]{1,0:T(8,128)(2,1)}, u32[]{:S(2)}) copy-start(bf16[2048,512]{1,0:T(8,128)(2,1)} %param.20) | copy-start | bytes 6291460
  766.0 12.9 %slice-start.4 = ((s8[5242880]{0:T(1024)(128)(4,1)}), s8[4194304]{0:T(1024)(128)(4,1)S(1)}, s32[]{:S(2)}) async-start(s8[5242880]{0:T(1024)(128)(4,1)} %bitcast.60), calls=%async_computation.7 | async-start | bytes 8388608
  766.0 12.9 %slice-start.6 = ((s8[5242880]{0:T(1024)(128)(4,1)}), s8[4194304]{0:T(1024)(128)(4,1)S(1)}, s32[]{:S(2)}) async-start(s8[5242880]{0:T(1024)(128)(4,1)} %bitcast.62), calls=%async_computation.9 | async-start | bytes 8388608
  788.2 9.3 %collective-permute-start.3 = (f32[4,10,256,1]{2,0,3,1:T(4,128)S(1)}, f32[4,10,256,1]{2,0,3,1:T(4,128)S(1)}, u32[]{:S(2)}, u32[]{:S(2)}) collective-permute-start(f32[4,10,256,1]{2,0,3,1:T(4,128)S(1)} %copy.22), channel_id=1, source_target_pairs={{0,8},{8,16},{16,24},{1,9},{9,17},{17,25},{2,10},{10,18},{18,26},{... | collective-permute-start | bytes 122888 | tf_op jit(solution)/shard_map/ppermute | solution.py:43
  795.5 5.6 collective-permute-start.4
  801.1 14.6 %slice-start.2 = ((s8[5242880]{0:T(1024)(128)(4,1)}), s8[1048576]{0:T(1024)(128)(4,1)S(1)}, s32[]{:S(2)}) async-start(s8[5242880]{0:T(1024)(128)(4,1)} %bitcast.58), calls=%async_computation.5 | async-start | bytes 2097152
  806.6 6.3 collective-permute-start.5
  809.7 6.0 collective-permute-start.6
  862.1 15.1 %copy-start.2 = (f32[10,258,514]{2,1,0:T(8,128)S(1)}, f32[10,258,514]{2,1,0:T(8,128)}, u32[]{:S(2)}) copy-start(f32[10,258,514]{2,1,0:T(8,128)} %get-tuple-element.14) | copy-start | bytes 15913444
  862.1 16.9 %copy-start.3 = (f32[10,258,514]{2,1,0:T(8,128)S(1)}, f32[10,258,514]{2,1,0:T(8,128)}, u32[]{:S(2)}) copy-start(f32[10,258,514]{2,1,0:T(8,128)} %get-tuple-element.15) | copy-start | bytes 15913444
  (11 other events, 101.3 us)
Sparse Core Ops, SparseCore 0:
  11.9 106.1 all-gather.3
  127.6 186.9 all-gather.5
  393.9 184.6 all-gather.7
